TPU v7x, 512 devices: a whole 4x8x8 slice. The times are simulated.
512 devices in a mesh: row: 16 (over y_lo, x), col: 32 (over z, y_hi, core).
Axes of the slice: x: 4, y: 8 (y_hi: 2, y_lo: 4; y = y_hi * 4 + y_lo), z: 8, core: 2. Of those that a mesh axis runs over, the one named last changes fastest.
Arguments:
- precond: float32 [8, 8192, 8192], P(None, 'row', 'col'), may hold values from -6 to 6
- out_factors: bfloat16 [1536, 8192], P('col', 'row'), may hold values from -6 to 6
- in_factors: bfloat16 [1536, 8192], P('row', 'col'), may hold values from -6 to 6
- token_mask: int32 [1536], replicated, may hold values 0 or 1
- seq_ids: int32 [1536], replicated, may hold values from 0 to 3, never falling along the last dimension, each value on 1 to 576 neighbouring positions
- query_ids: int32 [8], replicated, may hold values from 0 to 7, each once
Outputs:
- scores: float32 [8, 4], replicated
Inputs may be any that keep to these rules, and one draw needn't show every extreme that they name: seq_ids never falls along the tokens; each sequence has 1 to 576 tokens. query_ids names each query once.
All inputs are finite; a program needn't handle non-finite values.
Results may differ from a plain program's by a relative error of at most 0.0003.
Values may be sent and summed in bfloat16 or wider, within the bound.
No kernel may reach another device: no remote copies, remote signals or barrier semaphores. Data moves between devices by JAX's collectives and lax.ppermute only.
A program may use at most 64 MiB of HBM per device.

v0:
```python
import math

import jax
import jax.numpy as jnp
from jax import lax
from jax.sharding import PartitionSpec as P

DOUT = 8192
DIN = 8192
SEQ = 4
LEN = 384


def shards(precond, out_factors, in_factors, token_mask, seq_ids, query_ids):
    num_queries = precond.shape[0]
    weight = token_mask.astype(jnp.float32)[:, None] * (
        seq_ids[:, None] == jnp.arange(SEQ, dtype=jnp.int32)[None, :]
    ).astype(jnp.float32)
    out_whole = lax.all_gather(out_factors, "col", axis=0, tiled=True)
    out_wide = out_whole.astype(jnp.float32)
    in_wide = lax.all_gather(in_factors, "row", axis=0, tiled=True).astype(jnp.float32)

    def one_query(query_grad):
        mapped = lax.dot_general(
            in_wide, query_grad, (((1,), (1,)), ((), ())), precision=lax.Precision.HIGHEST
        )
        per_token = jnp.sum(mapped * out_wide, axis=1)
        return jnp.dot(per_token, weight, precision=lax.Precision.HIGHEST)

    total = lax.map(one_query, precond)
    summed = lax.psum(total, ("row", "col"))
    select = (query_ids[:, None] == jnp.arange(num_queries, dtype=jnp.int32)[None, :]).astype(
        jnp.float32
    )
    scale = 1.0 / math.sqrt(DOUT * DIN * LEN)
    return jnp.dot(select, summed, precision=lax.Precision.HIGHEST) * scale


def solution(mesh):
    placed = (P(None, "row", "col"), P("col", "row"), P("row", "col"), P(), P(), P())
    return jax.shard_map(shards, mesh=mesh, in_specs=placed, out_specs=P(), check_vma=False)
```

profile of v0, /device:TPU:1, one launch (start us, length us, event | category | flops | bytes accessed | tf_op | source)
XLA Modules:
  0.0 254.1 jit_solution(18171253237847577728)
XLA Ops:
  6.5 0.7 all-gather.2.cloned.1.call-update
  7.3 41.4 %all_gather.6 = bf16[1536,256]{1,0:T(8,128)(2,1)S(1)} all-gather(bf16[96,256]{1,0:T(8,128)(2,1)} %param.10), channel_id=1, replica_groups=mesh['row'=16,'col'=32] {'row'}, dimensions={0}, use_global_device_ids=true | all-gather | bytes 835584 | tf_op jit(solution)/shard_map/all_gather | solution.py:21
  48.7 1.3 convert_element_type.11
  50.0 55.2 %all-gather.2.cloned.1.call-done = bf16[1536,512]{1,0:T(8,128)(2,1)} async-done(((bf16[48,512]{1,0:T(8,128)(2,1)}), bf16[1536,512]{1,0:T(8,128)(2,1)}) %all-gather.2.cloned.1.call-update) | async-done | bytes 1572880 | tf_op jit(solution)/shard_map/all_gather | solution.py:19
  105.2 1.8 convert_element_type.12
  107.1 42.3 %while.11 = (s32[]{:T(128)}, f32[8,4]{1,0:T(8,128)S(1)}, f32[8,512,256]{2,1,0:T(8,128)}, f32[1536,256]{1,0:T(8,128)}, f32[1536,512]{1,0:T(8,128)S(1)}, /*index=5...) while((s32[]{:T(128)}, f32[8,4]{1,0:T(8,128)S(1)}, f32[8,512,256]{2,1,0:T(8,128)}, ...), condition=%wide.region_2.3_spmd.clone, body=%wide.region_0.2_spmd.clone.sunk | while | flops 2417576448 | bytes 5280401 | solution.py:30
  107.1 4.4 %fusion.27 = f32[1536]{0:T(1024)S(1)} fusion(f32[1536,512]{1,0:T(8,128)S(1)} %get-tuple-element.135, f32[1536,256]{1,0:T(8,128)} %get-tuple-element.134, f32[8,512,256]{2,1,0:T(8,128)} %get-tuple-element.133, s32[]{:T(128)} %get-tuple-element.122), kind=kOutput, calls=%fused_computation.3.clone.1 | convolution fusion | flops 2417490432 | bytes 5249536 | tf_op jit(solution)/shard_map/while/body/eval_jaxpr/dot_general | solution.py:24
  111.5 0.8 fusion.28
  112.4 4.4 %fusion.27 = f32[1536]{0:T(1024)S(1)} fusion(f32[1536,512]{1,0:T(8,128)S(1)} %get-tuple-element.135, f32[1536,256]{1,0:T(8,128)} %get-tuple-element.134, f32[8,512,256]{2,1,0:T(8,128)} %get-tuple-element.133, s32[]{:T(128)} %get-tuple-element.122), kind=kOutput, calls=%fused_computation.3.clone.1 | convolution fusion | flops 2417490432 | bytes 5249536 | tf_op jit(solution)/shard_map/while/body/eval_jaxpr/dot_general | solution.py:24
  116.8 0.8 fusion.28
  117.7 4.4 %fusion.27 = f32[1536]{0:T(1024)S(1)} fusion(f32[1536,512]{1,0:T(8,128)S(1)} %get-tuple-element.135, f32[1536,256]{1,0:T(8,128)} %get-tuple-element.134, f32[8,512,256]{2,1,0:T(8,128)} %get-tuple-element.133, s32[]{:T(128)} %get-tuple-element.122), kind=kOutput, calls=%fused_computation.3.clone.1 | convolution fusion | flops 2417490432 | bytes 5249536 | tf_op jit(solution)/shard_map/while/body/eval_jaxpr/dot_general | solution.py:24
  122.1 0.8 fusion.28
  123.0 4.4 %fusion.27 = f32[1536]{0:T(1024)S(1)} fusion(f32[1536,512]{1,0:T(8,128)S(1)} %get-tuple-element.135, f32[1536,256]{1,0:T(8,128)} %get-tuple-element.134, f32[8,512,256]{2,1,0:T(8,128)} %get-tuple-element.133, s32[]{:T(128)} %get-tuple-element.122), kind=kOutput, calls=%fused_computation.3.clone.1 | convolution fusion | flops 2417490432 | bytes 5249536 | tf_op jit(solution)/shard_map/while/body/eval_jaxpr/dot_general | solution.py:24
  127.4 0.8 fusion.28
  128.3 4.4 %fusion.27 = f32[1536]{0:T(1024)S(1)} fusion(f32[1536,512]{1,0:T(8,128)S(1)} %get-tuple-element.135, f32[1536,256]{1,0:T(8,128)} %get-tuple-element.134, f32[8,512,256]{2,1,0:T(8,128)} %get-tuple-element.133, s32[]{:T(128)} %get-tuple-element.122), kind=kOutput, calls=%fused_computation.3.clone.1 | convolution fusion | flops 2417490432 | bytes 5249536 | tf_op jit(solution)/shard_map/while/body/eval_jaxpr/dot_general | solution.py:24
  132.7 0.8 fusion.28
  133.6 4.4 %fusion.27 = f32[1536]{0:T(1024)S(1)} fusion(f32[1536,512]{1,0:T(8,128)S(1)} %get-tuple-element.135, f32[1536,256]{1,0:T(8,128)} %get-tuple-element.134, f32[8,512,256]{2,1,0:T(8,128)} %get-tuple-element.133, s32[]{:T(128)} %get-tuple-element.122), kind=kOutput, calls=%fused_computation.3.clone.1 | convolution fusion | flops 2417490432 | bytes 5249536 | tf_op jit(solution)/shard_map/while/body/eval_jaxpr/dot_general | solution.py:24
  138.0 0.8 fusion.28
  138.8 4.4 %fusion.27 = f32[1536]{0:T(1024)S(1)} fusion(f32[1536,512]{1,0:T(8,128)S(1)} %get-tuple-element.135, f32[1536,256]{1,0:T(8,128)} %get-tuple-element.134, f32[8,512,256]{2,1,0:T(8,128)} %get-tuple-element.133, s32[]{:T(128)} %get-tuple-element.122), kind=kOutput, calls=%fused_computation.3.clone.1 | convolution fusion | flops 2417490432 | bytes 5249536 | tf_op jit(solution)/shard_map/while/body/eval_jaxpr/dot_general | solution.py:24
  143.3 0.8 fusion.28
  144.1 4.4 %fusion.27 = f32[1536]{0:T(1024)S(1)} fusion(f32[1536,512]{1,0:T(8,128)S(1)} %get-tuple-element.135, f32[1536,256]{1,0:T(8,128)} %get-tuple-element.134, f32[8,512,256]{2,1,0:T(8,128)} %get-tuple-element.133, s32[]{:T(128)} %get-tuple-element.122), kind=kOutput, calls=%fused_computation.3.clone.1 | convolution fusion | flops 2417490432 | bytes 5249536 | tf_op jit(solution)/shard_map/while/body/eval_jaxpr/dot_general | solution.py:24
  148.5 0.8 fusion.28
  149.4 97.1 %psum.7 = f32[8,4]{1,0:T(8,128)S(1)} all-reduce(f32[8,4]{1,0:T(8,128)S(1)} %get-tuple-element.37), channel_id=1, replica_groups=mesh['row'=16,'col'=32] {'row','col'}, use_global_device_ids=true, to_apply=%region_3.4 | all-reduce | flops 32 | bytes 256 | tf_op jit(solution)/shard_map/psum | solution.py:31
  246.5 0.8 convolution_multiply_fusion
  (25 shorter events, 0.4 us)
Async XLA Ops:
  6.5 43.5 %copy-start = (s32[1536]{0:T(1024)S(1)}, s32[1536]{0:T(1024)}, u32[]{:S(2)}) copy-start(s32[1536]{0:T(1024)} %param.11) | copy-start | bytes 18436
  6.5 98.7 %all-gather.2.cloned.1.call-start = ((), (), s32[]{:S(2)}) async-start(), calls=%async_computation | async-start | bytes 1622016 | tf_op jit(solution)/shard_map/all_gather | solution.py:19
  48.7 58.4 %copy-start.1 = (s32[1536]{0:T(1024)S(1)}, s32[1536]{0:T(1024)}, u32[]{:S(2)}) copy-start(s32[1536]{0:T(1024)} %param.12) | copy-start | bytes 18436
  107.1 139.4 %copy-start.2 = (s32[8]{0:T(128)S(1)}, s32[8]{0:T(128)}, u32[]{:S(2)}) copy-start(s32[8]{0:T(128)} %param.13) | copy-start | bytes 100
Sparse Core Ops, SparseCore 0:
  10.7 94.5 all-gather.1
where the time goes:
time: 255 us; the launch traced here: 254 us
  blocking collectives  139 us (55%)
  waiting for transfers between devices  56 us (22%)
  matrix products  42.5 us (17%)
  between operations  13.4 us (5%)
  other arithmetic  3.12 us (1%)
    psum x1, blocking collectives, shards(): summed = lax.psum(total, ('row', 'col'))  97.1 us
    all_gather x1, waiting for transfers between devices, shards(): out_whole = lax.all_gather(out_factors, 'col', axis=0, tiled=True)  55.2 us
    all_gather x1, blocking collectives, shards(): lax.all_gather(in_factors, 'row', axis=0, tiled=True).astype(jnp.float32)  41.4 us
    dot_general x8, matrix products, one_query(): lax.dot_general(in_wide, query_grad, (((1,), (1,)), ((), ())), precision=...  35.2 us
    dot_general x8, matrix products, one_query(): return jnp.dot(per_token, weight, precision=lax.Precision.HIGHEST)  6.58 us
  transfers between devices with their start and end apart: 1, of which 1 were waited for; matrix products, arithmetic and copies ran while one was open for 1% of the time, Pallas kernels for 0%

commit v1 on v0

v1 whole, which is shorter than its diff:
```python
import math

import jax
import jax.numpy as jnp
from jax import lax
from jax.sharding import PartitionSpec as P

DOUT = 8192
DIN = 8192
SEQ = 4
LEN = 384
GATHER = "a2a"
FINAL = "a2a2"


def _gather(x, axis, size):
    if GATHER == "ag":
        return lax.all_gather(x, axis, axis=0, tiled=True)
    sent = jnp.broadcast_to(x[None], (size,) + x.shape)
    got = lax.all_to_all(sent, axis, 0, 0, tiled=True)
    return got.reshape((size * x.shape[0],) + x.shape[1:])


def _sum_over(x, axes, size):
    sent = jnp.broadcast_to(x[None], (size,) + x.shape)
    return lax.all_to_all(sent, axes, 0, 0, tiled=True).sum(0)


def shards(precond, out_factors, in_factors, token_mask, seq_ids, query_ids):
    num_queries = precond.shape[0]
    rows = lax.axis_size("row")
    cols = lax.axis_size("col")

    out_all = _gather(out_factors, "col", cols)
    in_all = _gather(in_factors, "row", rows)

    weight = token_mask.astype(jnp.float32)[:, None] * (
        seq_ids[:, None] == jnp.arange(SEQ, dtype=jnp.int32)[None, :]
    ).astype(jnp.float32)
    weighted = (weight.T[:, :, None] * out_all.astype(jnp.float32)[None]).astype(jnp.bfloat16)
    grad = lax.dot_general(
        weighted, in_all, (((1,), (0,)), ((), ())), preferred_element_type=jnp.float32
    )
    partial = lax.dot_general(
        precond, grad, (((1, 2), (1, 2)), ((), ())), precision=lax.Precision.HIGHEST
    )

    if FINAL == "psum":
        summed = lax.psum(partial, ("row", "col"))
    elif FINAL == "a2a1":
        summed = _sum_over(partial, ("row", "col"), rows * cols)
    else:
        summed = _sum_over(_sum_over(partial, "row", rows), "col", cols)

    select = (query_ids[:, None] == jnp.arange(num_queries, dtype=jnp.int32)[None, :]).astype(
        jnp.float32
    )
    scale = 1.0 / math.sqrt(DOUT * DIN * LEN)
    return jnp.dot(select, summed, precision=lax.Precision.HIGHEST) * scale


def solution(mesh):
    placed = (P(None, "row", "col"), P("col", "row"), P("row", "col"), P(), P(), P())
    return jax.shard_map(shards, mesh=mesh, in_specs=placed, out_specs=P(), check_vma=False)
```

time: 255 us -> 136 us (0.53)
  blocking collectives: 139 us -> 92.4 us
  waiting for transfers between devices: 56 us -> 13.5 us
  matrix products: 42.5 us -> 16.2 us
  between operations: 13.4 us -> 0.11 us
  starting transfers between devices: 0.01 us -> 7.02 us
  local copies, waits for them, and re-layouts: 0.35 us -> 4.33 us
    psum x1 -> x0, blocking collectives: 97.1 us -> none  [shards(): summed = lax.psum(total, ('row', 'col'))]
    all_to_all x0 -> x3, blocking collectives: none -> 92.4 us  [the longest x1 59.7 us: _gather(): got = lax.all_to_all(sent, axis, 0, 0, tiled=True)]
    all_gather x1 -> x0, waiting for transfers between devices: 55.2 us -> none  [shards(): out_whole = lax.all_gather(out_factors, 'col', axis=0, tiled=True)]
    all_gather x1 -> x0, blocking collectives: 41.4 us -> none  [shards(): lax.all_gather(in_factors, 'row', axis=0, tiled=True).astype(jnp.float32)]
    dot_general x16 -> x2, matrix products: 41.8 us -> 15.5 us  [the longest x1 11.4 us: shards(): lax.dot_general(precond, grad, (((1, 2), (1, 2)), ((), ())), precision=la...]
    all_to_all x0 -> x1, waiting for transfers between devices: none -> 13.5 us  [_gather(): got = lax.all_to_all(sent, axis, 0, 0, tiled=True)]
    all_to_all x0 -> x1, starting transfers between devices: none -> 7.02 us  [_gather(): got = lax.all_to_all(sent, axis, 0, 0, tiled=True)]
  transfers between devices with their start and end apart: 1 -> 1, of which waited for: 1 -> 1; matrix products, arithmetic and copies ran while one was open for 1% -> 3% of each run, Pallas kernels for 0% -> 0%
where the time goes in v1:
time: 136 us
  blocking collectives  92.4 us (68%)
  matrix products  16.2 us (12%)
  waiting for transfers between devices  13.5 us (10%)
  starting transfers between devices  7.02 us (5%)
  local copies, waits for them, and re-layouts  4.33 us (3%)
  other arithmetic  1.93 us (1%)
    all_to_all x1, blocking collectives, _gather(): got = lax.all_to_all(sent, axis, 0, 0, tiled=True)  59.7 us
    all_to_all x2, blocking collectives, _sum_over(): return lax.all_to_all(sent, axes, 0, 0, tiled=True).sum(0)  32.7 us
    all_to_all x1, waiting for transfers between devices, _gather(): got = lax.all_to_all(sent, axis, 0, 0, tiled=True)  13.5 us
    dot_general x1, matrix products, shards(): lax.dot_general(precond, grad, (((1, 2), (1, 2)), ((), ())), precision=la...  11.4 us
    all_to_all x1, starting transfers between devices, _gather(): got = lax.all_to_all(sent, axis, 0, 0, tiled=True)  7.02 us
    dot_general x1, matrix products, shards(): lax.dot_general(weighted, in_all, (((1,), (0,)), ((), ())), preferred_ele...  4.04 us
  transfers between devices with their start and end apart: 1, of which 1 were waited for; matrix products, arithmetic and copies ran while one was open for 3% of the time, Pallas kernels for 0%

profile of v1, /device:TPU:1, one launch (start us, length us, event | category | flops | bytes accessed | tf_op | source)
XLA Modules:
  0.0 135.6 jit_solution(8901247770299591413)
XLA Ops:
  0.0 0.0 copy-start.1
  0.0 1.0 broadcast_in_dim.8
  1.0 0.0 copy-start.3
  1.0 0.0 copy-start.2
  1.0 59.7 %all_to_all.20 = bf16[32,48,512]{2,1,0:T(8,128)(2,1)} all-to-all(bf16[32,48,512]{2,1,0:T(8,128)(2,1)S(1)} %broadcast_in_dim.8), channel_id=1, replica_groups=mesh['row'=16,'col'=32] {'col'}, dimensions={0} | all-to-all | bytes 3145728 | tf_op jit(solution)/shard_map/all_to_all | solution.py:20
  60.7 0.0 copy-done.1
  60.7 1.0 broadcast_in_dim.9
  61.7 7.0 %all-to-all-start.1 = ((bf16[16,96,256]{2,1,0:T(8,128)(2,1)}), bf16[16,96,256]{2,1,0:T(8,128)(2,1)}, u32[]{:S(2)}, u32[]{:S(2)}) async-start(bf16[16,96,256]{2,1,0:T(8,128)(2,1)} %broadcast_in_dim.9), calls=%async_computation.1 | async-start | bytes 1572864 | tf_op jit(solution)/shard_map/all_to_all | solution.py:20
  68.7 0.0 copy-done.3
  68.7 0.0 copy-done.2
  68.7 1.8 %bitcast_convert_fusion = f32[1536,512]{1,0:T(8,128)S(1)} fusion(bf16[32,48,512]{2,1,0:T(8,128)(2,1)} %all_to_all.20), kind=kLoop, calls=%fused_computation.7 | loop fusion | flops 786432 | bytes 4718592 | tf_op jit(solution)/shard_map/convert_element_type | solution.py:40
  70.6 2.4 %copy.11 = f32[1536,512]{0,1:T(8,128)} copy(f32[1536,512]{1,0:T(8,128)S(1)} %bitcast_convert_fusion) | data formatting | bytes 6291456 | tf_op jit(solution)/shard_map/convert_element_type | solution.py:40
  72.9 13.5 %all-to-all-done.1 = bf16[16,96,256]{2,1,0:T(8,128)(2,1)} async-done(((bf16[16,96,256]{2,1,0:T(8,128)(2,1)}), bf16[16,96,256]{2,1,0:T(8,128)(2,1)}, u32[]{:S(2)}, u32[]{:S(2)}) %all-to-all-start.1) | async-done | bytes 786464 | tf_op jit(solution)/shard_map/all_to_all | solution.py:20
  86.5 0.0 copy-start
  86.5 4.0 %fusion = f32[4,512,256]{2,1,0:T(8,128)S(1)} fusion(bf16[1536,256,1]{1,0,2:T(8,128)(2,1)} %bitcast.2, f32[1536,512]{0,1:T(8,128)} %copy.11, f32[4,1536]{1,0:T(4,128)S(1)} %fusion.11), kind=kOutput, calls=%fused_computation.1 | convolution fusion | flops 1616904192 | bytes 6053888 | tf_op jit(solution)/shard_map/dot_general | solution.py:41
  90.5 0.0 copy-done
  90.5 0.0 copy-start.4
  90.6 11.4 %fusion.6 = f32[8,4]{0,1:T(4,128)S(1)} fusion(f32[8,512,256]{2,1,0:T(8,128)S(1)} %copy-done, f32[4,512,256]{2,1,0:T(8,128)S(1)} %fusion), kind=kOutput, calls=%fused_computation.8 | convolution fusion | flops 50331648 | bytes 6291584 | tf_op jit(solution)/shard_map/dot_general | solution.py:44
  102.0 13.3 %all_to_all.21 = f32[16,8,4]{1,2,0:T(4,128)S(1)} all-to-all(f32[16,8,4]{1,2,0:T(4,128)S(1)} %broadcast_in_dim.10), channel_id=1, replica_groups=mesh['row'=16,'col'=32] {'row'}, dimensions={0} | all-to-all | bytes 4096 | tf_op jit(solution)/shard_map/all_to_all | solution.py:26
  115.4 19.4 %all_to_all.22 = f32[32,8,4]{1,2,0:T(4,128)S(1)} all-to-all(f32[32,8,4]{1,2,0:T(4,128)S(1)} %broadcast_in_dim.11), channel_id=1, replica_groups=mesh['row'=16,'col'=32] {'col'}, dimensions={0} | all-to-all | bytes 8192 | tf_op jit(solution)/shard_map/all_to_all | solution.py:26
  134.8 0.0 copy-done.4
  134.8 0.8 convolution_multiply_fusion
  (6 shorter events, 0.1 us)
Async XLA Ops:
  0.0 60.7 %copy-start.1 = (bf16[96,256]{1,0:T(8,128)(2,1)S(1)}, bf16[96,256]{1,0:T(8,128)(2,1)}, u32[]{:S(2)}) copy-start(bf16[96,256]{1,0:T(8,128)(2,1)} %param.8) | copy-start | bytes 147460
  1.0 67.7 %copy-start.3 = (s32[1536]{0:T(1024)S(1)}, s32[1536]{0:T(1024)}, u32[]{:S(2)}) copy-start(s32[1536]{0:T(1024)} %param.9) | copy-start | bytes 18436
  1.0 67.7 %copy-start.2 = (s32[1536]{0:T(1024)S(1)}, s32[1536]{0:T(1024)}, u32[]{:S(2)}) copy-start(s32[1536]{0:T(1024)} %param.10) | copy-start | bytes 18436
  61.7 24.8 %all-to-all-start.1 = ((bf16[16,96,256]{2,1,0:T(8,128)(2,1)}), bf16[16,96,256]{2,1,0:T(8,128)(2,1)}, u32[]{:S(2)}, u32[]{:S(2)}) async-start(bf16[16,96,256]{2,1,0:T(8,128)(2,1)} %broadcast_in_dim.9), calls=%async_computation.1 | async-start | bytes 1572864 | tf_op jit(solution)/shard_map/all_to_all | solution.py:20
  86.5 4.1 %copy-start = (f32[8,512,256]{2,1,0:T(8,128)S(1)}, f32[8,512,256]{2,1,0:T(8,128)}, u32[]{:S(2)}) copy-start(f32[8,512,256]{2,1,0:T(8,128)} %param.6) | copy-start | bytes 12582916
  90.5 44.3 %copy-start.4 = (s32[8]{0:T(128)S(1)}, s32[8]{0:T(128)}, u32[]{:S(2)}) copy-start(s32[8]{0:T(128)} %param.11) | copy-start | bytes 100

commit v2 on v1

v2 whole, which is shorter than its diff:
```python
import math

import jax
import jax.numpy as jnp
from jax import lax
from jax.sharding import Mesh, PartitionSpec as P

DOUT = 8192
DIN = 8192
SEQ = 4
LEN = 384
GATHER = "a2a"


def _gather(x, axis, size):
    if GATHER == "ag":
        return lax.all_gather(x, axis, axis=0, tiled=True)
    sent = jnp.broadcast_to(x[None], (size,) + x.shape)
    got = lax.all_to_all(sent, axis, 0, 0, tiled=True)
    return got.reshape((size * x.shape[0],) + x.shape[1:])


def _sum_over(x, axes, size):
    sent = jnp.broadcast_to(x[None], (size,) + x.shape)
    return lax.all_to_all(sent, axes, 0, 0, tiled=True).sum(0)


def shards(precond, out_factors, in_factors, token_mask, seq_ids, query_ids):
    num_queries = precond.shape[0]
    rows = lax.axis_size("row")
    cols = lax.axis_size("cg") * lax.axis_size("cc")

    groups = lax.axis_size("cg")
    cores = lax.axis_size("cc")
    core = lax.axis_index("cc")
    same = _gather(out_factors, "cg", groups).reshape((groups, 1) + out_factors.shape)
    other = lax.ppermute(same, "cc", [(0, 1), (1, 0)])
    out_all = jnp.concatenate([same, other], axis=1).reshape((-1, out_factors.shape[1]))
    in_all = _gather(in_factors, "row", rows)

    def in_our_order(x):
        y = x.reshape((groups, cores, x.shape[0] // (groups * cores)) + x.shape[1:])
        return jnp.where(core == 0, y, y[:, ::-1]).reshape(x.shape)

    in_all = in_our_order(in_all)
    weight = token_mask.astype(jnp.float32)[:, None] * (
        seq_ids[:, None] == jnp.arange(SEQ, dtype=jnp.int32)[None, :]
    ).astype(jnp.float32)
    weight = in_our_order(weight)
    weighted = weight.T.astype(jnp.bfloat16)[:, :, None] * in_all[None]
    grad = jnp.einsum("ti,stj->sij", out_all, weighted, preferred_element_type=jnp.float32)
    partial = jnp.sum(precond[:, None] * grad[None], axis=(2, 3))

    summed = _sum_over(_sum_over(partial, "row", rows), ("cg", "cc"), cols)

    select = (query_ids[:, None] == jnp.arange(num_queries, dtype=jnp.int32)[None, :]).astype(
        jnp.float32
    )
    scale = 1.0 / math.sqrt(DOUT * DIN * LEN)
    return jnp.dot(select, summed, precision=lax.Precision.HIGHEST) * scale


def solution(mesh):
    rows, cols = mesh.devices.shape
    split = Mesh(mesh.devices.reshape(rows, cols // 2, 2), ("row", "cg", "cc"))
    col = ("cg", "cc")
    placed = (P(None, "row", col), P(col, "row"), P("row", col), P(), P(), P())
    return jax.shard_map(shards, mesh=split, in_specs=placed, out_specs=P(), check_vma=False)
```

time: 136 us -> 111 us (0.82)
  blocking collectives: 92.4 us -> 68.4 us
  matrix products: 16.2 us -> 3.91 us
  starting transfers between devices: 7.02 us -> 15.9 us
  other arithmetic: 1.93 us -> 4.12 us
    all_to_all x1, blocking collectives: 59.7 us -> 36 us  [_gather(): got = lax.all_to_all(sent, axis, 0, 0, tiled=True)]
    dot_general x2 -> x1, matrix products: 15.5 us -> 3.13 us  [shards(): jnp.einsum('ti,stj->sij', out_all, weighted, preferred_element_type=jnp.f...]
    all_to_all x1, starting transfers between devices: 7.02 us -> 12.5 us  [_gather(): got = lax.all_to_all(sent, axis, 0, 0, tiled=True)]
    reduce_sum x0 -> x1, other arithmetic: none -> 3.66 us  [shards(): partial = jnp.sum(precond[:, None] * grad[None], axis=(2, 3))]
    ppermute x0 -> x1, starting transfers between devices: none -> 3.42 us  [shards(): other = lax.ppermute(same, 'cc', [(0, 1), (1, 0)])]
    convert_element_type x1, local copies, waits for them, and re-layouts: 2.36 us -> 0.11 us  [shards(): weighted = weight.T.astype(jnp.bfloat16)[:, :, None] * in_all[None]]
    transpose x0 -> x1, local copies, waits for them, and re-layouts: none -> 1.92 us  [shards(): jnp.einsum('ti,stj->sij', out_all, weighted, preferred_element_type=jnp.f...]
    convert_element_type x1, other arithmetic: 1.84 us -> 0.05 us  [shards(): weighted = weight.T.astype(jnp.bfloat16)[:, :, None] * in_all[None]]
  transfers between devices with their start and end apart: 1 -> 2, of which waited for: 1 -> 1; matrix products, arithmetic and copies ran while one was open for 3% -> 1% of each run, Pallas kernels for 0% -> 0%
where the time goes in v2:
time: 111 us
  blocking collectives  68.4 us (62%)
  starting transfers between devices  15.9 us (14%)
  waiting for transfers between devices  13.7 us (12%)
  local copies, waits for them, and re-layouts  4.58 us (4%)
  other arithmetic  4.12 us (4%)
  matrix products  3.91 us (4%)
    all_to_all x1, blocking collectives, _gather(): got = lax.all_to_all(sent, axis, 0, 0, tiled=True)  36 us
    all_to_all x2, blocking collectives, _sum_over(): return lax.all_to_all(sent, axes, 0, 0, tiled=True).sum(0)  32.3 us
    all_to_all x1, waiting for transfers between devices, _gather(): got = lax.all_to_all(sent, axis, 0, 0, tiled=True)  13.7 us
    all_to_all x1, starting transfers between devices, _gather(): got = lax.all_to_all(sent, axis, 0, 0, tiled=True)  12.5 us
    reduce_sum x1, other arithmetic, shards(): partial = jnp.sum(precond[:, None] * grad[None], axis=(2, 3))  3.66 us
    ppermute x1, starting transfers between devices, shards(): other = lax.ppermute(same, 'cc', [(0, 1), (1, 0)])  3.42 us
    dot_general x1, matrix products, shards(): jnp.einsum('ti,stj->sij', out_all, weighted, preferred_element_type=jnp.f...  3.13 us
  transfers between devices with their start and end apart: 2, of which 1 were waited for; matrix products, arithmetic and copies ran while one was open for 1% of the time, Pallas kernels for 0%

profile of v2, /device:TPU:1, one launch (start us, length us, event | category | flops | bytes accessed | tf_op | source)
XLA Modules:
  0.0 110.8 jit_solution(8081965552432903360)
XLA Ops:
  0.0 0.9 broadcast_in_dim.9
  0.9 0.0 copy-start.2
  0.9 0.0 copy-start.1
  0.9 36.0 %all_to_all.20 = bf16[16,48,512]{2,1,0:T(8,128)(2,1)S(1)} all-to-all(bf16[16,48,512]{2,1,0:T(8,128)(2,1)S(1)} %broadcast_in_dim.9), channel_id=1, replica_groups=mesh['row'=16,'cg'=16,'cc'=2] {'cg'}, dimensions={0} | all-to-all | bytes 1572864 | tf_op jit(solution)/shard_map/all_to_all | solution.py:19
  37.0 1.0 broadcast_in_dim.8
  37.9 12.5 %all-to-all-start = ((bf16[16,96,256]{2,1,0:T(8,128)(2,1)}), bf16[16,96,256]{2,1,0:T(8,128)(2,1)S(1)}, u32[]{:S(2)}, u32[]{:S(2)}) async-start(bf16[16,96,256]{2,1,0:T(8,128)(2,1)} %broadcast_in_dim.8), calls=%async_computation | async-start | bytes 1572864 | tf_op jit(solution)/shard_map/all_to_all | solution.py:19
  50.4 3.4 %collective-permute-start = (bf16[16,1,48,512]{3,2,1,0:T(8,128)(2,1)S(1)}, bf16[16,1,48,512]{3,2,1,0:T(8,128)(2,1)S(1)}, u32[]{:S(2)}, u32[]{:S(2)}) collective-permute-start(bf16[16,1,48,512]{3,2,1,0:T(8,128)(2,1)S(1)} %bitcast.15), channel_id=1, source_target_pairs={{0,1},{1,0},{2,3},{3,2},{4,5},{5,4},{6,7},{7,6},{8,9},{9,8},{10,11... | collective-permute-start | bytes 2359304 | tf_op jit(solution)/shard_map/ppermute | solution.py:37
  53.8 0.1 mul.45
  53.9 0.1 eq.37
  54.1 0.2 rev.6
  54.3 0.1 convert_element_type.16
  54.4 13.7 %all-to-all-done = bf16[16,96,256]{2,1,0:T(8,128)(2,1)S(1)} async-done(((bf16[16,96,256]{2,1,0:T(8,128)(2,1)}), bf16[16,96,256]{2,1,0:T(8,128)(2,1)S(1)}, u32[]{:S(2)}, u32[]{:S(2)}) %all-to-all-start) | async-done | bytes 786464 | tf_op jit(solution)/shard_map/all_to_all | solution.py:19
  68.1 0.1 reverse_select_fusion
  68.3 0.3 copy.15
  68.6 0.0 collective-permute-done
  68.6 0.2 pad_maximum_fusion
  68.7 3.1 %fusion.2 = f32[4,512,256]{1,2,0:T(8,128)} fusion(bf16[1536,512,1]{1,0,2:T(8,128)(2,1)S(1)} %bitcast.17, bf16[1536,256]{0,1:T(8,128)(2,1)S(1)} %copy.15, bf16[4,1536]{1,0:T(4,128)(2,1)S(1)} %bitcast.18), kind=kOutput, calls=%fused_computation.3 | convolution fusion | flops 1612185600 | bytes 4468736 | tf_op jit(solution)/shard_map/ti,stj->sij/dot_general | solution.py:51
  71.9 1.9 %copy.16 = f32[4,512,256]{2,1,0:T(8,128)S(1)} copy(f32[4,512,256]{1,2,0:T(8,128)} %fusion.2) | data formatting | bytes 4194304 | tf_op jit(solution)/shard_map/ti,stj->sij/transpose | solution.py:51
  73.8 0.0 copy-start.3
  73.8 3.7 %multiply_reduce_fusion = f32[8,4]{1,0:T(8,128)S(1)} fusion(f32[4,512,256]{2,1,0:T(8,128)S(1)} %copy.16, f32[8,512,256]{2,1,0:T(8,128)} %param.6), kind=kLoop, calls=%fused_computation | loop fusion | flops 8388576 | bytes 6291584 | tf_op jit(solution)/shard_map/reduce_sum | solution.py:52
  77.5 0.1 copy.17
  77.6 13.3 %all_to_all.21 = f32[16,8,4]{1,2,0:T(4,128)S(1)} all-to-all(f32[16,8,4]{1,2,0:T(4,128)S(1)} %broadcast_in_dim.10), channel_id=1, replica_groups=mesh['row'=16,'cg'=16,'cc'=2] {'row'}, dimensions={0} | all-to-all | bytes 4096 | tf_op jit(solution)/shard_map/all_to_all | solution.py:25
  90.9 19.0 %all_to_all.22 = f32[32,8,4]{1,2,0:T(4,128)S(1)} all-to-all(f32[32,8,4]{1,2,0:T(4,128)S(1)} %broadcast_in_dim.11), channel_id=1, replica_groups=mesh['row'=16,'cg'=16,'cc'=2] {'cg','cc'}, dimensions={0} | all-to-all | bytes 8192 | tf_op jit(solution)/shard_map/all_to_all | solution.py:25
  110.0 0.8 convolution_multiply_fusion
  (12 shorter events, 0.2 us)
Async XLA Ops:
  0.0 37.0 %copy-start = (bf16[96,256]{1,0:T(8,128)(2,1)S(1)}, bf16[96,256]{1,0:T(8,128)(2,1)}, u32[]{:S(2)}) copy-start(bf16[96,256]{1,0:T(8,128)(2,1)} %param.8) | copy-start | bytes 147460
  0.9 52.9 %copy-start.2 = (s32[1536]{0:T(1024)S(1)}, s32[1536]{0:T(1024)}, u32[]{:S(2)}) copy-start(s32[1536]{0:T(1024)} %param.9) | copy-start | bytes 18436
  0.9 53.0 %copy-start.1 = (s32[1536]{0:T(1024)S(1)}, s32[1536]{0:T(1024)}, u32[]{:S(2)}) copy-start(s32[1536]{0:T(1024)} %param.10) | copy-start | bytes 18436
  37.9 30.2 %all-to-all-start = ((bf16[16,96,256]{2,1,0:T(8,128)(2,1)}), bf16[16,96,256]{2,1,0:T(8,128)(2,1)S(1)}, u32[]{:S(2)}, u32[]{:S(2)}) async-start(bf16[16,96,256]{2,1,0:T(8,128)(2,1)} %broadcast_in_dim.8), calls=%async_computation | async-start | bytes 1572864 | tf_op jit(solution)/shard_map/all_to_all | solution.py:19
  50.4 18.2 %collective-permute-start = (bf16[16,1,48,512]{3,2,1,0:T(8,128)(2,1)S(1)}, bf16[16,1,48,512]{3,2,1,0:T(8,128)(2,1)S(1)}, u32[]{:S(2)}, u32[]{:S(2)}) collective-permute-start(bf16[16,1,48,512]{3,2,1,0:T(8,128)(2,1)S(1)} %bitcast.15), channel_id=1, source_target_pairs={{0,1},{1,0},{2,3},{3,2},{4,5},{5,4},{6,7},{7,6},{8,9},{9,8},{10,11... | collective-permute-start | bytes 2359304 | tf_op jit(solution)/shard_map/ppermute | solution.py:37
  73.8 36.2 %copy-start.3 = (s32[8]{0:T(128)S(1)}, s32[8]{0:T(128)}, u32[]{:S(2)}) copy-start(s32[8]{0:T(128)} %param.11) | copy-start | bytes 100

commit v3 on v2

--- a/solution.py
+++ b/solution.py
@@ -47,11 +47,11 @@
         seq_ids[:, None] == jnp.arange(SEQ, dtype=jnp.int32)[None, :]
     ).astype(jnp.float32)
     weight = in_our_order(weight)
-    weighted = weight.T.astype(jnp.bfloat16)[:, :, None] * in_all[None]
-    grad = jnp.einsum("ti,stj->sij", out_all, weighted, preferred_element_type=jnp.float32)
+    weighted = weight.T.astype(jnp.bfloat16)[:, :, None] * out_all[None]
+    grad = jnp.einsum("sti,tj->sij", weighted, in_all, preferred_element_type=jnp.float32)
     partial = jnp.sum(precond[:, None] * grad[None], axis=(2, 3))
 
-    summed = _sum_over(_sum_over(partial, "row", rows), ("cg", "cc"), cols)
+    summed = _sum_over(_sum_over(partial, ("row", "cc"), rows * cores), "cg", groups)
 
     select = (query_ids[:, None] == jnp.arange(num_queries, dtype=jnp.int32)[None, :]).astype(
         jnp.float32

time: 111 us -> 107 us (0.964)
  blocking collectives: 68.4 us -> 67 us
  local copies, waits for them, and re-layouts: 4.58 us -> 3.21 us
  other arithmetic: 4.12 us -> 2.99 us
    reduce_sum x1, other arithmetic: 3.66 us -> 1.65 us  [shards(): partial = jnp.sum(precond[:, None] * grad[None], axis=(2, 3))]
    transpose x1 -> x0, local copies, waits for them, and re-layouts: 1.92 us -> none  [shards(): jnp.einsum('ti,stj->sij', out_all, weighted, preferred_element_type=jnp.f...]
    all_to_all x2, blocking collectives: 32.3 us -> 31 us  [_sum_over(): return lax.all_to_all(sent, axes, 0, 0, tiled=True).sum(0)]
where the time goes in v3:
time: 107 us
  blocking collectives  67 us (63%)
  starting transfers between devices  15.9 us (15%)
  waiting for transfers between devices  13.7 us (13%)
  matrix products  3.89 us (4%)
  local copies, waits for them, and re-layouts  3.21 us (3%)
  other arithmetic  2.99 us (3%)
    all_to_all x1, blocking collectives, _gather(): got = lax.all_to_all(sent, axis, 0, 0, tiled=True)  36 us
    all_to_all x2, blocking collectives, _sum_over(): return lax.all_to_all(sent, axes, 0, 0, tiled=True).sum(0)  31 us
    all_to_all x1, waiting for transfers between devices, _gather(): got = lax.all_to_all(sent, axis, 0, 0, tiled=True)  13.7 us
    all_to_all x1, starting transfers between devices, _gather(): got = lax.all_to_all(sent, axis, 0, 0, tiled=True)  12.5 us
    ppermute x1, starting transfers between devices, shards(): other = lax.ppermute(same, 'cc', [(0, 1), (1, 0)])  3.42 us
    dot_general x1, matrix products, shards(): jnp.einsum('sti,tj->sij', weighted, in_all, preferred_element_type=jnp.fl...  3.12 us
  transfers between devices with their start and end apart: 2, of which 1 were waited for; matrix products, arithmetic and copies ran while one was open for 1% of the time, Pallas kernels for 0%

profile of v3, /device:TPU:1, one launch (start us, length us, event | category | flops | bytes accessed | tf_op | source)
XLA Modules:
  0.0 106.9 jit_solution(8865949657955828958)
XLA Ops:
  0.0 0.9 broadcast_in_dim.8
  0.9 0.0 copy-start.3
  0.9 0.0 copy-start.2
  0.9 36.0 %all_to_all.20 = bf16[16,48,512]{2,1,0:T(8,128)(2,1)S(1)} all-to-all(bf16[16,48,512]{2,1,0:T(8,128)(2,1)S(1)} %broadcast_in_dim.8), channel_id=1, replica_groups=mesh['row'=16,'cg'=16,'cc'=2] {'cg'}, dimensions={0} | all-to-all | bytes 1572864 | tf_op jit(solution)/shard_map/all_to_all | solution.py:19
  37.0 1.0 broadcast_in_dim.9
  37.9 12.5 %all-to-all-start.1 = ((bf16[16,96,256]{2,1,0:T(8,128)(2,1)}), bf16[16,96,256]{2,1,0:T(8,128)(2,1)S(1)}, u32[]{:S(2)}, u32[]{:S(2)}) async-start(bf16[16,96,256]{2,1,0:T(8,128)(2,1)} %broadcast_in_dim.9), calls=%async_computation.1 | async-start | bytes 1572864 | tf_op jit(solution)/shard_map/all_to_all | solution.py:19
  50.4 3.4 %collective-permute-start = (bf16[16,1,48,512]{3,2,0,1:T(8,128)(2,1)S(1)}, bf16[16,1,48,512]{3,2,0,1:T(8,128)(2,1)S(1)}, u32[]{:S(2)}, u32[]{:S(2)}) collective-permute-start(bf16[16,1,48,512]{3,2,0,1:T(8,128)(2,1)S(1)} %bitcast.13), channel_id=1, source_target_pairs={{0,1},{1,0},{2,3},{3,2},{4,5},{5,4},{6,7},{7,6},{8,9},{9,8},{10,11... | collective-permute-start | bytes 2359304 | tf_op jit(solution)/shard_map/ppermute | solution.py:37
  53.8 0.1 mul.45
  53.9 0.1 eq.37
  54.1 0.2 rev.6
  54.3 0.1 convert_element_type.16
  54.4 13.7 %all-to-all-done.1 = bf16[16,96,256]{2,1,0:T(8,128)(2,1)S(1)} async-done(((bf16[16,96,256]{2,1,0:T(8,128)(2,1)}), bf16[16,96,256]{2,1,0:T(8,128)(2,1)S(1)}, u32[]{:S(2)}, u32[]{:S(2)}) %all-to-all-start.1) | async-done | bytes 786464 | tf_op jit(solution)/shard_map/all_to_all | solution.py:19
  68.1 1.0 reverse_select_fusion
  69.2 0.1 pad_maximum_fusion
  69.3 0.1 copy.12
  69.4 0.7 copy.13
  70.1 0.0 copy-start
  70.1 3.1 %fusion = f32[4,512,256]{2,1,0:T(8,128)S(1)} fusion(bf16[1536,256,1]{1,0,2:T(8,128)(2,1)} %bitcast.15, bf16[1536,512]{0,1:T(8,128)(2,1)S(1)} %copy.13, bf16[4,1536]{1,0:T(4,128)(2,1)S(1)} %bitcast.16), kind=kOutput, calls=%fused_computation.1 | convolution fusion | flops 1613758464 | bytes 4468736 | tf_op jit(solution)/shard_map/sti,tj->sij/dot_general | solution.py:51
  73.3 0.0 copy-start.4
  73.3 1.7 %multiply_reduce_fusion = f32[8,4]{1,0:T(8,128)S(1)} fusion(f32[4,512,256]{2,1,0:T(8,128)S(1)} %fusion, f32[8,512,256]{2,1,0:T(8,128)S(1)} %copy-done), kind=kLoop, calls=%fused_computation | loop fusion | flops 8388576 | bytes 6291584 | tf_op jit(solution)/shard_map/reduce_sum | solution.py:52
  74.9 0.1 copy.14
  75.0 16.1 %all_to_all.21 = f32[32,8,4]{1,2,0:T(4,128)S(1)} all-to-all(f32[32,8,4]{1,2,0:T(4,128)S(1)} %broadcast_in_dim.10), channel_id=1, replica_groups=mesh['row'=16,'cg'=16,'cc'=2] {'row','cc'}, dimensions={0} | all-to-all | bytes 8192 | tf_op jit(solution)/shard_map/all_to_all | solution.py:25
  91.2 14.8 %all_to_all.22 = f32[16,8,4]{1,2,0:T(4,128)S(1)} all-to-all(f32[16,8,4]{1,2,0:T(4,128)S(1)} %broadcast_in_dim.11), channel_id=1, replica_groups=mesh['row'=16,'cg'=16,'cc'=2] {'cg'}, dimensions={0} | all-to-all | bytes 4096 | tf_op jit(solution)/shard_map/all_to_all | solution.py:25
  106.1 0.8 convolution_multiply_fusion
  (14 shorter events, 0.2 us)
Async XLA Ops:
  0.0 37.0 %copy-start.1 = (bf16[96,256]{1,0:T(8,128)(2,1)S(1)}, bf16[96,256]{1,0:T(8,128)(2,1)}, u32[]{:S(2)}) copy-start(bf16[96,256]{1,0:T(8,128)(2,1)} %param.8) | copy-start | bytes 147460
  0.9 52.9 %copy-start.3 = (s32[1536]{0:T(1024)S(1)}, s32[1536]{0:T(1024)}, u32[]{:S(2)}) copy-start(s32[1536]{0:T(1024)} %param.9) | copy-start | bytes 18436
  0.9 53.0 %copy-start.2 = (s32[1536]{0:T(1024)S(1)}, s32[1536]{0:T(1024)}, u32[]{:S(2)}) copy-start(s32[1536]{0:T(1024)} %param.10) | copy-start | bytes 18436
  37.9 30.2 %all-to-all-start.1 = ((bf16[16,96,256]{2,1,0:T(8,128)(2,1)}), bf16[16,96,256]{2,1,0:T(8,128)(2,1)S(1)}, u32[]{:S(2)}, u32[]{:S(2)}) async-start(bf16[16,96,256]{2,1,0:T(8,128)(2,1)} %broadcast_in_dim.9), calls=%async_computation.1 | async-start | bytes 1572864 | tf_op jit(solution)/shard_map/all_to_all | solution.py:19
  50.4 18.8 %collective-permute-start = (bf16[16,1,48,512]{3,2,0,1:T(8,128)(2,1)S(1)}, bf16[16,1,48,512]{3,2,0,1:T(8,128)(2,1)S(1)}, u32[]{:S(2)}, u32[]{:S(2)}) collective-permute-start(bf16[16,1,48,512]{3,2,0,1:T(8,128)(2,1)S(1)} %bitcast.13), channel_id=1, source_target_pairs={{0,1},{1,0},{2,3},{3,2},{4,5},{5,4},{6,7},{7,6},{8,9},{9,8},{10,11... | collective-permute-start | bytes 2359304 | tf_op jit(solution)/shard_map/ppermute | solution.py:37
  70.1 3.1 %copy-start = (f32[8,512,256]{2,1,0:T(8,128)S(1)}, f32[8,512,256]{2,1,0:T(8,128)}, u32[]{:S(2)}) copy-start(f32[8,512,256]{2,1,0:T(8,128)} %param.6) | copy-start | bytes 12582916
  73.3 32.8 %copy-start.4 = (s32[8]{0:T(128)S(1)}, s32[8]{0:T(128)}, u32[]{:S(2)}) copy-start(s32[8]{0:T(128)} %param.11) | copy-start | bytes 100

commit v4 on v3

--- a/solution.py
+++ b/solution.py
@@ -28,12 +28,12 @@
 def shards(precond, out_factors, in_factors, token_mask, seq_ids, query_ids):
     num_queries = precond.shape[0]
     rows = lax.axis_size("row")
-    cols = lax.axis_size("cg") * lax.axis_size("cc")
+    cols = lax.axis_size("cz") * lax.axis_size("cy") * lax.axis_size("cc")
 
-    groups = lax.axis_size("cg")
+    groups = lax.axis_size("cz") * lax.axis_size("cy")
     cores = lax.axis_size("cc")
     core = lax.axis_index("cc")
-    same = _gather(out_factors, "cg", groups).reshape((groups, 1) + out_factors.shape)
+    same = _gather(out_factors, ("cz", "cy"), groups).reshape((groups, 1) + out_factors.shape)
     other = lax.ppermute(same, "cc", [(0, 1), (1, 0)])
     out_all = jnp.concatenate([same, other], axis=1).reshape((-1, out_factors.shape[1]))
     in_all = _gather(in_factors, "row", rows)
@@ -51,7 +51,8 @@
     grad = jnp.einsum("sti,tj->sij", weighted, in_all, preferred_element_type=jnp.float32)
     partial = jnp.sum(precond[:, None] * grad[None], axis=(2, 3))
 
-    summed = _sum_over(_sum_over(partial, ("row", "cc"), rows * cores), "cg", groups)
+    near = rows * cores * lax.axis_size("cy")
+    summed = _sum_over(_sum_over(partial, ("row", "cy", "cc"), near), "cz", lax.axis_size("cz"))
 
     select = (query_ids[:, None] == jnp.arange(num_queries, dtype=jnp.int32)[None, :]).astype(
         jnp.float32
@@ -62,7 +63,7 @@
 
 def solution(mesh):
     rows, cols = mesh.devices.shape
-    split = Mesh(mesh.devices.reshape(rows, cols // 2, 2), ("row", "cg", "cc"))
-    col = ("cg", "cc")
+    split = Mesh(mesh.devices.reshape(rows, cols // 4, 2, 2), ("row", "cz", "cy", "cc"))
+    col = ("cz", "cy", "cc")
     placed = (P(None, "row", col), P(col, "row"), P("row", col), P(), P(), P())
     return jax.shard_map(shards, mesh=split, in_specs=placed, out_specs=P(), check_vma=False)

time: 107 us -> 105 us (0.981)
  blocking collectives: 67 us -> 65 us
    all_to_all x2, blocking collectives: 31 us -> 29 us  [_sum_over(): return lax.all_to_all(sent, axes, 0, 0, tiled=True).sum(0)]
where the time goes in v4:
time: 105 us
  blocking collectives  65 us (62%)
  starting transfers between devices  15.9 us (15%)
  waiting for transfers between devices  13.7 us (13%)
  matrix products  3.89 us (4%)
  local copies, waits for them, and re-layouts  3.21 us (3%)
  other arithmetic  3.01 us (3%)
    all_to_all x1, blocking collectives, _gather(): got = lax.all_to_all(sent, axis, 0, 0, tiled=True)  36 us
    all_to_all x2, blocking collectives, _sum_over(): return lax.all_to_all(sent, axes, 0, 0, tiled=True).sum(0)  29 us
    all_to_all x1, waiting for transfers between devices, _gather(): got = lax.all_to_all(sent, axis, 0, 0, tiled=True)  13.7 us
    all_to_all x1, starting transfers between devices, _gather(): got = lax.all_to_all(sent, axis, 0, 0, tiled=True)  12.5 us
    ppermute x1, starting transfers between devices, shards(): other = lax.ppermute(same, 'cc', [(0, 1), (1, 0)])  3.42 us
    dot_general x1, matrix products, shards(): jnp.einsum('sti,tj->sij', weighted, in_all, preferred_element_type=jnp.fl...  3.12 us
  transfers between devices with their start and end apart: 2, of which 1 were waited for; matrix products, arithmetic and copies ran while one was open for 1% of the time, Pallas kernels for 0%

profile of v4, /device:TPU:1, one launch (start us, length us, event | category | flops | bytes accessed | tf_op | source)
XLA Modules:
  0.0 104.9 jit_solution(8976790740408339017)
XLA Ops:
  0.0 0.9 broadcast_in_dim.8
  0.9 0.0 copy-start.3
  0.9 0.0 copy-start.2
  0.9 36.0 %all_to_all.20 = bf16[16,48,512]{2,1,0:T(8,128)(2,1)S(1)} all-to-all(bf16[16,48,512]{2,1,0:T(8,128)(2,1)S(1)} %broadcast_in_dim.8), channel_id=1, replica_groups=mesh['row'=16,'cz'=8,'cy'=2,'cc'=2] {'cz','cy'}, dimensions={0} | all-to-all | bytes 1572864 | tf_op jit(solution)/shard_map/all_to_all | solution.py:19
  37.0 1.0 broadcast_in_dim.9
  37.9 12.5 %all-to-all-start.1 = ((bf16[16,96,256]{2,1,0:T(8,128)(2,1)}), bf16[16,96,256]{2,1,0:T(8,128)(2,1)S(1)}, u32[]{:S(2)}, u32[]{:S(2)}) async-start(bf16[16,96,256]{2,1,0:T(8,128)(2,1)} %broadcast_in_dim.9), calls=%async_computation.1 | async-start | bytes 1572864 | tf_op jit(solution)/shard_map/all_to_all | solution.py:19
  50.4 3.4 %collective-permute-start = (bf16[16,1,48,512]{3,2,0,1:T(8,128)(2,1)S(1)}, bf16[16,1,48,512]{3,2,0,1:T(8,128)(2,1)S(1)}, u32[]{:S(2)}, u32[]{:S(2)}) collective-permute-start(bf16[16,1,48,512]{3,2,0,1:T(8,128)(2,1)S(1)} %bitcast.13), channel_id=1, source_target_pairs={{0,1},{1,0},{2,3},{3,2},{4,5},{5,4},{6,7},{7,6},{8,9},{9,8},{10,11... | collective-permute-start | bytes 2359304 | tf_op jit(solution)/shard_map/ppermute | solution.py:37
  53.8 0.1 mul.45
  53.9 0.1 eq.37
  54.1 0.2 rev.6
  54.3 0.1 convert_element_type.16
  54.4 13.7 %all-to-all-done.1 = bf16[16,96,256]{2,1,0:T(8,128)(2,1)S(1)} async-done(((bf16[16,96,256]{2,1,0:T(8,128)(2,1)}), bf16[16,96,256]{2,1,0:T(8,128)(2,1)S(1)}, u32[]{:S(2)}, u32[]{:S(2)}) %all-to-all-start.1) | async-done | bytes 786464 | tf_op jit(solution)/shard_map/all_to_all | solution.py:19
  68.1 1.0 reverse_select_fusion
  69.2 0.1 pad_maximum_fusion
  69.3 0.1 copy.12
  69.4 0.7 copy.13
  70.1 0.0 copy-start
  70.1 3.1 %fusion = f32[4,512,256]{2,1,0:T(8,128)S(1)} fusion(bf16[1536,256,1]{1,0,2:T(8,128)(2,1)} %bitcast.15, bf16[1536,512]{0,1:T(8,128)(2,1)S(1)} %copy.13, bf16[4,1536]{1,0:T(4,128)(2,1)S(1)} %bitcast.16), kind=kOutput, calls=%fused_computation.1 | convolution fusion | flops 1613758464 | bytes 4468736 | tf_op jit(solution)/shard_map/sti,tj->sij/dot_general | solution.py:51
  73.3 1.7 %multiply_reduce_fusion = f32[8,4]{1,0:T(8,128)S(1)} fusion(f32[4,512,256]{2,1,0:T(8,128)S(1)} %fusion, f32[8,512,256]{2,1,0:T(8,128)S(1)} %copy-done), kind=kLoop, calls=%fused_computation | loop fusion | flops 8388576 | bytes 6291584 | tf_op jit(solution)/shard_map/reduce_sum | solution.py:52
  74.9 0.1 copy.14
  75.1 19.7 %all_to_all.21 = f32[64,8,4]{1,2,0:T(4,128)S(1)} all-to-all(f32[64,8,4]{1,2,0:T(4,128)S(1)} %broadcast_in_dim.10), channel_id=1, replica_groups=mesh['row'=16,'cz'=8,'cy'=2,'cc'=2] {'row','cy','cc'}, dimensions={0} | all-to-all | bytes 16384 | tf_op jit(solution)/shard_map/all_to_all | solution.py:25
  94.7 0.1 reduce_sum.28
  94.8 9.3 %all_to_all.22 = f32[8,8,4]{1,2,0:T(4,128)S(1)} all-to-all(f32[8,8,4]{1,2,0:T(4,128)S(1)} %broadcast_in_dim.11), channel_id=1, replica_groups=mesh['row'=16,'cz'=8,'cy'=2,'cc'=2] {'cz'}, dimensions={0} | all-to-all | bytes 2048 | tf_op jit(solution)/shard_map/all_to_all | solution.py:25
  104.2 0.8 convolution_multiply_fusion
  (14 shorter events, 0.2 us)
Async XLA Ops:
  0.0 37.0 %copy-start.1 = (bf16[96,256]{1,0:T(8,128)(2,1)S(1)}, bf16[96,256]{1,0:T(8,128)(2,1)}, u32[]{:S(2)}) copy-start(bf16[96,256]{1,0:T(8,128)(2,1)} %param.8) | copy-start | bytes 147460
  0.9 52.9 %copy-start.3 = (s32[1536]{0:T(1024)S(1)}, s32[1536]{0:T(1024)}, u32[]{:S(2)}) copy-start(s32[1536]{0:T(1024)} %param.9) | copy-start | bytes 18436
  0.9 53.0 %copy-start.2 = (s32[1536]{0:T(1024)S(1)}, s32[1536]{0:T(1024)}, u32[]{:S(2)}) copy-start(s32[1536]{0:T(1024)} %param.10) | copy-start | bytes 18436
  37.9 30.2 %all-to-all-start.1 = ((bf16[16,96,256]{2,1,0:T(8,128)(2,1)}), bf16[16,96,256]{2,1,0:T(8,128)(2,1)S(1)}, u32[]{:S(2)}, u32[]{:S(2)}) async-start(bf16[16,96,256]{2,1,0:T(8,128)(2,1)} %broadcast_in_dim.9), calls=%async_computation.1 | async-start | bytes 1572864 | tf_op jit(solution)/shard_map/all_to_all | solution.py:19
  50.4 18.8 %collective-permute-start = (bf16[16,1,48,512]{3,2,0,1:T(8,128)(2,1)S(1)}, bf16[16,1,48,512]{3,2,0,1:T(8,128)(2,1)S(1)}, u32[]{:S(2)}, u32[]{:S(2)}) collective-permute-start(bf16[16,1,48,512]{3,2,0,1:T(8,128)(2,1)S(1)} %bitcast.13), channel_id=1, source_target_pairs={{0,1},{1,0},{2,3},{3,2},{4,5},{5,4},{6,7},{7,6},{8,9},{9,8},{10,11... | collective-permute-start | bytes 2359304 | tf_op jit(solution)/shard_map/ppermute | solution.py:37
  70.1 3.1 %copy-start = (f32[8,512,256]{2,1,0:T(8,128)S(1)}, f32[8,512,256]{2,1,0:T(8,128)}, u32[]{:S(2)}) copy-start(f32[8,512,256]{2,1,0:T(8,128)} %param.6) | copy-start | bytes 12582916
  73.3 30.9 %copy-start.4 = (s32[8]{0:T(128)S(1)}, s32[8]{0:T(128)}, u32[]{:S(2)}) copy-start(s32[8]{0:T(128)} %param.11) | copy-start | bytes 100

commit v5 on v4

--- a/solution.py
+++ b/solution.py
@@ -35,18 +35,13 @@
     core = lax.axis_index("cc")
     same = _gather(out_factors, ("cz", "cy"), groups).reshape((groups, 1) + out_factors.shape)
     other = lax.ppermute(same, "cc", [(0, 1), (1, 0)])
-    out_all = jnp.concatenate([same, other], axis=1).reshape((-1, out_factors.shape[1]))
+    out_all = jnp.where(
+        core == 0, jnp.concatenate([same, other], axis=1), jnp.concatenate([other, same], axis=1)
+    ).reshape((-1, out_factors.shape[1]))
     in_all = _gather(in_factors, "row", rows)
-
-    def in_our_order(x):
-        y = x.reshape((groups, cores, x.shape[0] // (groups * cores)) + x.shape[1:])
-        return jnp.where(core == 0, y, y[:, ::-1]).reshape(x.shape)
-
-    in_all = in_our_order(in_all)
     weight = token_mask.astype(jnp.float32)[:, None] * (
         seq_ids[:, None] == jnp.arange(SEQ, dtype=jnp.int32)[None, :]
     ).astype(jnp.float32)
-    weight = in_our_order(weight)
     weighted = weight.T.astype(jnp.bfloat16)[:, :, None] * out_all[None]
     grad = jnp.einsum("sti,tj->sij", weighted, in_all, preferred_element_type=jnp.float32)
     partial = jnp.sum(precond[:, None] * grad[None], axis=(2, 3))

time: 105 us -> 103 us (0.981)
    all_to_all x1, waiting for transfers between devices: 13.7 us -> 11.4 us  [_gather(): got = lax.all_to_all(sent, axis, 0, 0, tiled=True)]
    ppermute x1, waiting for transfers between devices: 0.01 us -> 1.83 us  [shards(): other = lax.ppermute(same, 'cc', [(0, 1), (1, 0)])]
  transfers between devices with their start and end apart: 2 -> 2, of which waited for: 1 -> 2; matrix products, arithmetic and copies ran while one was open for 1% -> 1% of each run, Pallas kernels for 0% -> 0%
where the time goes in v5:
time: 103 us
  blocking collectives  65 us (63%)
  starting transfers between devices  15.9 us (15%)
  waiting for transfers between devices  13.2 us (13%)
  matrix products  3.89 us (4%)
  local copies, waits for them, and re-layouts  2.84 us (3%)
  other arithmetic  2.02 us (2%)
    all_to_all x1, blocking collectives, _gather(): got = lax.all_to_all(sent, axis, 0, 0, tiled=True)  36 us
    all_to_all x2, blocking collectives, _sum_over(): return lax.all_to_all(sent, axes, 0, 0, tiled=True).sum(0)  29 us
    all_to_all x1, starting transfers between devices, _gather(): got = lax.all_to_all(sent, axis, 0, 0, tiled=True)  12.5 us
    all_to_all x1, waiting for transfers between devices, _gather(): got = lax.all_to_all(sent, axis, 0, 0, tiled=True)  11.4 us
    ppermute x1, starting transfers between devices, shards(): other = lax.ppermute(same, 'cc', [(0, 1), (1, 0)])  3.42 us
    dot_general x1, matrix products, shards(): jnp.einsum('sti,tj->sij', weighted, in_all, preferred_element_type=jnp.fl...  3.11 us
  transfers between devices with their start and end apart: 2, of which 2 were waited for; matrix products, arithmetic and copies ran while one was open for 1% of the time, Pallas kernels for 0%

profile of v5, /device:TPU:1, one launch (start us, length us, event | category | flops | bytes accessed | tf_op | source)
XLA Modules:
  0.0 103.0 jit_solution(9763110666082415124)
XLA Ops:
  0.0 0.9 broadcast_in_dim.8
  0.9 0.0 copy-start.3
  0.9 0.0 copy-start.2
  0.9 36.0 %all_to_all.20 = bf16[16,48,512]{2,1,0:T(8,128)(2,1)S(1)} all-to-all(bf16[16,48,512]{2,1,0:T(8,128)(2,1)S(1)} %broadcast_in_dim.8), channel_id=1, replica_groups=mesh['row'=16,'cz'=8,'cy'=2,'cc'=2] {'cz','cy'}, dimensions={0} | all-to-all | bytes 1572864 | tf_op jit(solution)/shard_map/all_to_all | solution.py:19
  36.9 0.0 copy-done.1
  37.0 1.0 broadcast_in_dim.9
  37.9 12.5 %all-to-all-start.1 = ((bf16[16,96,256]{2,1,0:T(8,128)(2,1)}), bf16[16,96,256]{2,1,0:T(8,128)(2,1)}, u32[]{:S(2)}, u32[]{:S(2)}) async-start(bf16[16,96,256]{2,1,0:T(8,128)(2,1)} %broadcast_in_dim.9), calls=%async_computation.1 | async-start | bytes 1572864 | tf_op jit(solution)/shard_map/all_to_all | solution.py:19
  50.5 3.4 %collective-permute-start = (bf16[16,1,48,512]{3,2,0,1:T(8,128)(2,1)S(1)}, bf16[16,1,48,512]{3,2,0,1:T(8,128)(2,1)S(1)}, u32[]{:S(2)}, u32[]{:S(2)}) collective-permute-start(bf16[16,1,48,512]{3,2,0,1:T(8,128)(2,1)S(1)} %bitcast.8), channel_id=1, source_target_pairs={{0,1},{1,0},{2,3},{3,2},{4,5},{5,4},{6,7},{7,6},{8,9},{9,8},{10,11... | collective-permute-start | bytes 2359304 | tf_op jit(solution)/shard_map/ppermute | solution.py:37
  53.9 0.0 copy-done.3
  53.9 0.0 copy-done.2
  53.9 1.8 %collective-permute-done = bf16[16,1,48,512]{3,2,0,1:T(8,128)(2,1)S(1)} collective-permute-done((bf16[16,1,48,512]{3,2,0,1:T(8,128)(2,1)S(1)}, bf16[16,1,48,512]{3,2,0,1:T(8,128)(2,1)S(1)}, u32[]{:S(2)}, u32[]{:S(2)}) %collective-permute-start) | collective-permute-done | bytes 786464 | tf_op jit(solution)/shard_map/ppermute | solution.py:37
  55.8 0.3 maximum_select_fusion
  56.0 0.1 copy.10
  56.2 0.7 copy.11
  56.9 11.4 %all-to-all-done.1 = bf16[16,96,256]{2,1,0:T(8,128)(2,1)} async-done(((bf16[16,96,256]{2,1,0:T(8,128)(2,1)}), bf16[16,96,256]{2,1,0:T(8,128)(2,1)}, u32[]{:S(2)}, u32[]{:S(2)}) %all-to-all-start.1) | async-done | bytes 786464 | tf_op jit(solution)/shard_map/all_to_all | solution.py:19
  68.3 3.1 %fusion = f32[4,512,256]{2,1,0:T(8,128)S(1)} fusion(bf16[1536,256,1]{1,0,2:T(8,128)(2,1)} %bitcast.3, bf16[1536,512]{0,1:T(8,128)(2,1)S(1)} %copy.11, bf16[4,1536]{1,0:T(4,128)(2,1)S(1)} %select_convert_fusion), kind=kOutput, calls=%fused_computation.1 | convolution fusion | flops 1613758464 | bytes 4468736 | tf_op jit(solution)/shard_map/sti,tj->sij/dot_general | solution.py:46
  71.4 0.0 copy-done
  71.4 0.0 copy-start.4
  71.4 1.7 %multiply_reduce_fusion = f32[8,4]{1,0:T(8,128)S(1)} fusion(f32[4,512,256]{2,1,0:T(8,128)S(1)} %fusion, f32[8,512,256]{2,1,0:T(8,128)S(1)} %copy-done), kind=kLoop, calls=%fused_computation | loop fusion | flops 8388576 | bytes 6291584 | tf_op jit(solution)/shard_map/reduce_sum | solution.py:47
  73.1 0.1 copy.12
  73.2 19.7 %all_to_all.21 = f32[64,8,4]{1,2,0:T(4,128)S(1)} all-to-all(f32[64,8,4]{1,2,0:T(4,128)S(1)} %broadcast_in_dim.10), channel_id=1, replica_groups=mesh['row'=16,'cz'=8,'cy'=2,'cc'=2] {'row','cy','cc'}, dimensions={0} | all-to-all | bytes 16384 | tf_op jit(solution)/shard_map/all_to_all | solution.py:25
  92.8 0.1 reduce_sum.28
  92.9 9.3 %all_to_all.22 = f32[8,8,4]{1,2,0:T(4,128)S(1)} all-to-all(f32[8,8,4]{1,2,0:T(4,128)S(1)} %broadcast_in_dim.11), channel_id=1, replica_groups=mesh['row'=16,'cz'=8,'cy'=2,'cc'=2] {'cz'}, dimensions={0} | all-to-all | bytes 2048 | tf_op jit(solution)/shard_map/all_to_all | solution.py:25
  102.3 0.8 convolution_multiply_fusion
  (8 shorter events, 0.1 us)
Async XLA Ops:
  0.0 37.0 %copy-start.1 = (bf16[96,256]{1,0:T(8,128)(2,1)S(1)}, bf16[96,256]{1,0:T(8,128)(2,1)}, u32[]{:S(2)}) copy-start(bf16[96,256]{1,0:T(8,128)(2,1)} %param.8) | copy-start | bytes 147460
  0.9 53.0 %copy-start.3 = (s32[1536]{0:T(1024)S(1)}, s32[1536]{0:T(1024)}, u32[]{:S(2)}) copy-start(s32[1536]{0:T(1024)} %param.9) | copy-start | bytes 18436
  0.9 53.0 %copy-start.2 = (s32[1536]{0:T(1024)S(1)}, s32[1536]{0:T(1024)}, u32[]{:S(2)}) copy-start(s32[1536]{0:T(1024)} %param.10) | copy-start | bytes 18436
  37.9 30.3 %all-to-all-start.1 = ((bf16[16,96,256]{2,1,0:T(8,128)(2,1)}), bf16[16,96,256]{2,1,0:T(8,128)(2,1)}, u32[]{:S(2)}, u32[]{:S(2)}) async-start(bf16[16,96,256]{2,1,0:T(8,128)(2,1)} %broadcast_in_dim.9), calls=%async_computation.1 | async-start | bytes 1572864 | tf_op jit(solution)/shard_map/all_to_all | solution.py:19
  50.5 5.3 %collective-permute-start = (bf16[16,1,48,512]{3,2,0,1:T(8,128)(2,1)S(1)}, bf16[16,1,48,512]{3,2,0,1:T(8,128)(2,1)S(1)}, u32[]{:S(2)}, u32[]{:S(2)}) collective-permute-start(bf16[16,1,48,512]{3,2,0,1:T(8,128)(2,1)S(1)} %bitcast.8), channel_id=1, source_target_pairs={{0,1},{1,0},{2,3},{3,2},{4,5},{5,4},{6,7},{7,6},{8,9},{9,8},{10,11... | collective-permute-start | bytes 2359304 | tf_op jit(solution)/shard_map/ppermute | solution.py:37
  68.3 3.1 %copy-start = (f32[8,512,256]{2,1,0:T(8,128)S(1)}, f32[8,512,256]{2,1,0:T(8,128)}, u32[]{:S(2)}) copy-start(f32[8,512,256]{2,1,0:T(8,128)} %param.6) | copy-start | bytes 12582916
  71.4 30.9 %copy-start.4 = (s32[8]{0:T(128)S(1)}, s32[8]{0:T(128)}, u32[]{:S(2)}) copy-start(s32[8]{0:T(128)} %param.11) | copy-start | bytes 100

commit v6 on v5

--- a/solution.py
+++ b/solution.py
@@ -49,11 +49,8 @@
     near = rows * cores * lax.axis_size("cy")
     summed = _sum_over(_sum_over(partial, ("row", "cy", "cc"), near), "cz", lax.axis_size("cz"))
 
-    select = (query_ids[:, None] == jnp.arange(num_queries, dtype=jnp.int32)[None, :]).astype(
-        jnp.float32
-    )
     scale = 1.0 / math.sqrt(DOUT * DIN * LEN)
-    return jnp.dot(select, summed, precision=lax.Precision.HIGHEST) * scale
+    return jnp.take(summed, query_ids, axis=0) * scale
 
 
 def solution(mesh):

time: 103 us -> 106 us (1.029)
  blocking collectives: 65 us -> 36.2 us
  waiting for transfers between devices: 13.2 us -> 30.6 us
  starting transfers between devices: 15.9 us -> 28.2 us
  local copies, waits for them, and re-layouts: 2.84 us -> 5.35 us
    all_to_all x2 -> x0, blocking collectives: 29 us -> none  [_sum_over(): return lax.all_to_all(sent, axes, 0, 0, tiled=True).sum(0)]
    all_to_all x0 -> x2, waiting for transfers between devices: none -> 17.4 us  [_sum_over(): return lax.all_to_all(sent, axes, 0, 0, tiled=True).sum(0)]
    all_to_all x0 -> x2, starting transfers between devices: none -> 12.3 us  [_sum_over(): return lax.all_to_all(sent, axes, 0, 0, tiled=True).sum(0)]
    broadcast_in_dim x2, local copies, waits for them, and re-layouts: 0.03 us -> 1.27 us  [_sum_over(): sent = jnp.broadcast_to(x[None], (size,) + x.shape)]
  transfers between devices with their start and end apart: 2 -> 4, of which waited for: 2 -> 4; matrix products, arithmetic and copies ran while one was open for 1% -> 1% of each run, Pallas kernels for 0% -> 0%
where the time goes in v6:
time: 106 us
  blocking collectives  36.2 us (34%)
  waiting for transfers between devices  30.6 us (29%)
  starting transfers between devices  28.2 us (27%)
  local copies, waits for them, and re-layouts  5.35 us (5%)
  matrix products  3.12 us (3%)
  other arithmetic  2.11 us (2%)
    all_to_all x1, blocking collectives, _gather(): got = lax.all_to_all(sent, axis, 0, 0, tiled=True)  36.2 us
    all_to_all x2, waiting for transfers between devices, _sum_over(): return lax.all_to_all(sent, axes, 0, 0, tiled=True).sum(0)  17.4 us
    all_to_all x1, starting transfers between devices, _gather(): got = lax.all_to_all(sent, axis, 0, 0, tiled=True)  12.5 us
    all_to_all x2, starting transfers between devices, _sum_over(): return lax.all_to_all(sent, axes, 0, 0, tiled=True).sum(0)  12.3 us
    all_to_all x1, waiting for transfers between devices, _gather(): got = lax.all_to_all(sent, axis, 0, 0, tiled=True)  11.4 us
    ppermute x1, starting transfers between devices, shards(): other = lax.ppermute(same, 'cc', [(0, 1), (1, 0)])  3.42 us
    dot_general x1, matrix products, shards(): jnp.einsum('sti,tj->sij', weighted, in_all, preferred_element_type=jnp.fl...  3.12 us
  transfers between devices with their start and end apart: 4, of which 4 were waited for; matrix products, arithmetic and copies ran while one was open for 1% of the time, Pallas kernels for 0%

profile of v6, /device:TPU:1, one launch (start us, length us, event | category | flops | bytes accessed | tf_op | source)
XLA Modules:
  0.0 105.8 jit_solution(8243622392552401200)
XLA Ops:
  0.0 0.9 broadcast_in_dim.18
  0.9 36.2 %all_to_all.20 = bf16[16,48,512]{2,1,0:T(8,128)(2,1)S(1)} all-to-all(bf16[16,48,512]{2,1,0:T(8,128)(2,1)S(1)} %broadcast_in_dim.18), channel_id=1, replica_groups=mesh['row'=16,'cz'=8,'cy'=2,'cc'=2] {'cz','cy'}, dimensions={0} | all-to-all | bytes 1572864 | tf_op jit(solution)/shard_map/all_to_all | solution.py:19
  37.1 1.0 broadcast_in_dim.19
  38.1 12.5 %all-to-all-start.1 = ((bf16[16,96,256]{2,1,0:T(8,128)(2,1)}), bf16[16,96,256]{2,1,0:T(8,128)(2,1)}, u32[]{:S(2)}, u32[]{:S(2)}) async-start(bf16[16,96,256]{2,1,0:T(8,128)(2,1)} %broadcast_in_dim.19), calls=%async_computation.1 | async-start | bytes 1572864 | tf_op jit(solution)/shard_map/all_to_all | solution.py:19
  50.6 3.4 %collective-permute-start = (bf16[16,1,48,512]{3,2,0,1:T(8,128)(2,1)S(1)}, bf16[16,1,48,512]{3,2,0,1:T(8,128)(2,1)S(1)}, u32[]{:S(2)}, u32[]{:S(2)}) collective-permute-start(bf16[16,1,48,512]{3,2,0,1:T(8,128)(2,1)S(1)} %bitcast.7), channel_id=1, source_target_pairs={{0,1},{1,0},{2,3},{3,2},{4,5},{5,4},{6,7},{7,6},{8,9},{9,8},{10,11... | collective-permute-start | bytes 2359304 | tf_op jit(solution)/shard_map/ppermute | solution.py:37
  54.1 1.8 %collective-permute-done = bf16[16,1,48,512]{3,2,0,1:T(8,128)(2,1)S(1)} collective-permute-done((bf16[16,1,48,512]{3,2,0,1:T(8,128)(2,1)S(1)}, bf16[16,1,48,512]{3,2,0,1:T(8,128)(2,1)S(1)}, u32[]{:S(2)}, u32[]{:S(2)}) %collective-permute-start) | collective-permute-done | bytes 786464 | tf_op jit(solution)/shard_map/ppermute | solution.py:37
  55.9 0.3 maximum_select_fusion
  56.2 0.1 copy.19
  56.3 0.7 copy.20
  57.0 11.4 %all-to-all-done.1 = bf16[16,96,256]{2,1,0:T(8,128)(2,1)} async-done(((bf16[16,96,256]{2,1,0:T(8,128)(2,1)}), bf16[16,96,256]{2,1,0:T(8,128)(2,1)}, u32[]{:S(2)}, u32[]{:S(2)}) %all-to-all-start.1) | async-done | bytes 786464 | tf_op jit(solution)/shard_map/all_to_all | solution.py:19
  68.4 3.1 %fusion = f32[4,512,256]{2,1,0:T(8,128)S(1)} fusion(bf16[1536,256,1]{1,0,2:T(8,128)(2,1)} %bitcast.3, bf16[1536,512]{0,1:T(8,128)(2,1)S(1)} %copy.20, bf16[4,1536]{1,0:T(4,128)(2,1)S(1)} %select_convert_fusion), kind=kOutput, calls=%fused_computation.2 | convolution fusion | flops 1613758464 | bytes 4468736 | tf_op jit(solution)/shard_map/sti,tj->sij/dot_general | solution.py:46
  71.5 1.7 %multiply_reduce_fusion = f32[8,4]{1,0:T(8,128)S(1)} fusion(f32[4,512,256]{2,1,0:T(8,128)S(1)} %fusion, f32[8,512,256]{2,1,0:T(8,128)S(1)} %copy-done), kind=kLoop, calls=%fused_computation.1 | loop fusion | flops 8388576 | bytes 6291584 | tf_op jit(solution)/shard_map/reduce_sum | solution.py:47
  73.2 0.1 copy.21
  73.3 0.7 broadcast_in_dim.20
  73.9 9.0 %all-to-all-start.2 = ((f32[64,8,4]{1,2,0:T(4,128)}), f32[64,8,4]{1,2,0:T(4,128)S(1)}, u32[]{:S(2)}, u32[]{:S(2)}) async-start(f32[64,8,4]{1,2,0:T(4,128)} %broadcast_in_dim.20), calls=%async_computation.2 | async-start | bytes 262144 | tf_op jit(solution)/shard_map/all_to_all | solution.py:25
  82.9 10.9 %all-to-all-done.2 = f32[64,8,4]{1,2,0:T(4,128)S(1)} async-done(((f32[64,8,4]{1,2,0:T(4,128)}), f32[64,8,4]{1,2,0:T(4,128)S(1)}, u32[]{:S(2)}, u32[]{:S(2)}) %all-to-all-start.2) | async-done | bytes 8224 | tf_op jit(solution)/shard_map/all_to_all | solution.py:25
  93.8 0.1 reduce_sum.28
  93.9 0.6 broadcast_in_dim.21
  94.5 3.3 %all-to-all-start.3 = ((f32[8,8,4]{1,2,0:T(4,128)}), f32[8,8,4]{1,2,0:T(4,128)S(1)}, u32[]{:S(2)}, u32[]{:S(2)}) async-start(f32[8,8,4]{1,2,0:T(4,128)} %broadcast_in_dim.21), calls=%async_computation.3 | async-start | bytes 32768 | tf_op jit(solution)/shard_map/all_to_all | solution.py:25
  97.8 6.5 %all-to-all-done.3 = f32[8,8,4]{1,2,0:T(4,128)S(1)} async-done(((f32[8,8,4]{1,2,0:T(4,128)}), f32[8,8,4]{1,2,0:T(4,128)S(1)}, u32[]{:S(2)}, u32[]{:S(2)}) %all-to-all-start.3) | async-done | bytes 1056 | tf_op jit(solution)/shard_map/all_to_all | solution.py:25
  104.4 0.1 copy.22
  104.5 0.6 gather_fusion
  105.0 0.1 select_multiply_fusion
  105.1 0.7 copy.23
  (16 shorter events, 0.1 us)
Async XLA Ops:
  0.0 37.1 %copy-start.1 = (bf16[96,256]{1,0:T(8,128)(2,1)S(1)}, bf16[96,256]{1,0:T(8,128)(2,1)}, u32[]{:S(2)}) copy-start(bf16[96,256]{1,0:T(8,128)(2,1)} %param.8) | copy-start | bytes 147460
  0.9 53.1 %copy-start.3 = (s32[1536]{0:T(1024)S(1)}, s32[1536]{0:T(1024)}, u32[]{:S(2)}) copy-start(s32[1536]{0:T(1024)} %param.9) | copy-start | bytes 18436
  0.9 53.1 %copy-start.4 = (s32[8]{0:T(128)S(1)}, s32[8]{0:T(128)}, u32[]{:S(2)}) copy-start(s32[8]{0:T(128)} %param.11) | copy-start | bytes 100
  0.9 53.2 %copy-start.2 = (s32[1536]{0:T(1024)S(1)}, s32[1536]{0:T(1024)}, u32[]{:S(2)}) copy-start(s32[1536]{0:T(1024)} %param.10) | copy-start | bytes 18436
  38.1 30.3 %all-to-all-start.1 = ((bf16[16,96,256]{2,1,0:T(8,128)(2,1)}), bf16[16,96,256]{2,1,0:T(8,128)(2,1)}, u32[]{:S(2)}, u32[]{:S(2)}) async-start(bf16[16,96,256]{2,1,0:T(8,128)(2,1)} %broadcast_in_dim.19), calls=%async_computation.1 | async-start | bytes 1572864 | tf_op jit(solution)/shard_map/all_to_all | solution.py:19
  50.6 5.3 %collective-permute-start = (bf16[16,1,48,512]{3,2,0,1:T(8,128)(2,1)S(1)}, bf16[16,1,48,512]{3,2,0,1:T(8,128)(2,1)S(1)}, u32[]{:S(2)}, u32[]{:S(2)}) collective-permute-start(bf16[16,1,48,512]{3,2,0,1:T(8,128)(2,1)S(1)} %bitcast.7), channel_id=1, source_target_pairs={{0,1},{1,0},{2,3},{3,2},{4,5},{5,4},{6,7},{7,6},{8,9},{9,8},{10,11... | collective-permute-start | bytes 2359304 | tf_op jit(solution)/shard_map/ppermute | solution.py:37
  68.4 3.1 %copy-start = (f32[8,512,256]{2,1,0:T(8,128)S(1)}, f32[8,512,256]{2,1,0:T(8,128)}, u32[]{:S(2)}) copy-start(f32[8,512,256]{2,1,0:T(8,128)} %param.6) | copy-start | bytes 12582916
  73.9 19.9 %all-to-all-start.2 = ((f32[64,8,4]{1,2,0:T(4,128)}), f32[64,8,4]{1,2,0:T(4,128)S(1)}, u32[]{:S(2)}, u32[]{:S(2)}) async-start(f32[64,8,4]{1,2,0:T(4,128)} %broadcast_in_dim.20), calls=%async_computation.2 | async-start | bytes 262144 | tf_op jit(solution)/shard_map/all_to_all | solution.py:25
  94.5 9.9 %all-to-all-start.3 = ((f32[8,8,4]{1,2,0:T(4,128)}), f32[8,8,4]{1,2,0:T(4,128)S(1)}, u32[]{:S(2)}, u32[]{:S(2)}) async-start(f32[8,8,4]{1,2,0:T(4,128)} %broadcast_in_dim.21), calls=%async_computation.3 | async-start | bytes 32768 | tf_op jit(solution)/shard_map/all_to_all | solution.py:25
